TPU v7x, 32 devices: a whole 2x2x4 slice. The times are simulated.
32 devices in a mesh: groups: 2 (over y), frames: 4 (over z), heads: 4 (over x, core).
Axes of the slice: x: 2, y: 2, z: 4, core: 2. Of those that a mesh axis runs over, the one named last changes fastest.
Arguments:
- query_heads: bfloat16 [16384, 896], P(('groups', 'frames'), 'heads'), parts along dimension 0, may hold values from -6 to 6
- key_heads: bfloat16 [16384, 896], P(('groups', 'frames'), 'heads'), parts along dimension 0, may hold values from -0.04 to 8
- value_heads: bfloat16 [16384, 896], P(('groups', 'frames'), 'heads'), parts along dimension 0, may hold values from -6 to 6
- residual: bfloat16 [16384, 2240], P(('groups', 'frames', 'heads')), parts along dimension 0, may hold values from -6 to 6
- out_proj: bfloat16 [896, 2240], P('frames'), may hold values from -0.1875 to 0.1875
- frame_gate: float32 [32, 2240], P(('groups', 'frames')), parts along dimension 0, may hold values from -4 to 4
Outputs:
- updated: bfloat16 [16384, 2240], P(('groups', 'frames', 'heads')), parts along dimension 0
There are 2 independent parts, one for each index of `groups`. A program takes and returns all parts, laid end to end along the dimension named above; an argument that names none is the same for every part. Nothing has to cross between parts.
All inputs are finite; a program needn't handle non-finite values.
Results may differ from a plain program's by a relative error of at most 0.0033.
Values may be sent and summed in bfloat16 or wider, within the bound.
No kernel may reach another device: no remote copies, remote signals or barrier semaphores. Data moves between devices by JAX's collectives and lax.ppermute only.
A program may use at most 64 MiB of HBM per device.

v0:
```python
import jax
import jax.numpy as jnp
from jax import lax
from jax.sharding import PartitionSpec as P

HD = 112
FRAME_TOK = 512


EPSILON = 1e-06


def _exclusive_prefix(x, nf):
    if nf <= 8:
        total = jnp.zeros_like(x)
        for d in range(1, nf):
            total = total + lax.ppermute(x, "frames", [(i, i + d) for i in range(nf - d)])
        return total
    y = lax.ppermute(x, "frames", [(i, i + 1) for i in range(nf - 1)])
    covered = 1
    while covered < nf - 1:
        y = y + lax.ppermute(y, "frames", [(i, i + covered) for i in range(nf - covered)])
        covered *= 2
    return y


def _ring_out_proj(out_proj, nf, nh, ng):
    rows, _ = out_proj.shape
    sub = rows // (2 * ng)
    g = lax.axis_index("groups")
    core = lax.axis_index("heads") % 2
    shares = [jnp.remainder(g - s, ng) * 2 + core for s in range(ng)]
    shares += [jnp.remainder(g - s, ng) * 2 + 1 - core for s in range(ng)]
    pieces = [lax.dynamic_slice_in_dim(out_proj, share * sub, sub, axis=0) for share in shares]
    swap = [(a, a ^ 1) for a in range(nh)]
    fetched = []
    for t in range(1, nf):
        fetched.append(lax.ppermute(pieces[0], "frames", [(i, (i + t) % nf) for i in range(nf)]))
    fetched = jnp.stack(fetched)
    from_groups = [fetched] + [
        lax.ppermute(fetched, "groups", [(a, (a + s) % ng) for a in range(ng)])
        for s in range(1, ng)
    ]
    mine = jnp.stack(from_groups, axis=1)
    theirs = lax.ppermute(mine, "heads", swap)
    for t in range(nf - 1):
        pieces += [mine[t, s] for s in range(ng)] + [theirs[t, s] for s in range(ng)]
    return jnp.concatenate(pieces, axis=0), jnp.stack(shares)


def make_per_device(nf, nh, ng):
    def per_device(query_heads, key_heads, value_heads, residual, out_proj, frame_gate):
        weights, shares = _ring_out_proj(out_proj, nf, nh, ng)
        attended = _attend(query_heads, key_heads, value_heads, nf)
        return _project(attended, weights, shares, residual, frame_gate, nf, ng)

    return per_device


def _attend(query_heads, key_heads, value_heads, nf):
    length, width = query_heads.shape
    frames_here = length // FRAME_TOK
    heads_here = width // HD
    block_shape = (frames_here, FRAME_TOK, width)
    query_pos = jnp.maximum(query_heads, 0).reshape(block_shape)
    key_pos = jnp.maximum(key_heads, 0).reshape(block_shape)
    value_frames = value_heads.reshape(block_shape)
    lane_head = jnp.arange(width, dtype=jnp.int32) // HD
    same_head = lane_head[:, None] == lane_head[None, :]

    frame_state = jnp.einsum(
        "fti,ftj->fij", key_pos, value_frames, preferred_element_type=jnp.float32
    )
    frame_state = jnp.where(same_head[None], frame_state, 0.0)
    frame_sum = jnp.sum(key_pos, axis=1, dtype=jnp.float32)
    own_state = jnp.sum(frame_state, axis=0)
    own_sum = jnp.sum(frame_sum, axis=0)

    blocks = [
        own_state[a * HD:(a + 1) * HD, a * HD:(a + 1) * HD] for a in range(heads_here)
    ]
    compact = jnp.concatenate(
        [jnp.stack(blocks), own_sum.reshape(heads_here, 1, HD)], axis=1
    )
    earlier = _exclusive_prefix(compact, nf)
    eye = jnp.eye(heads_here, dtype=jnp.float32)
    earlier_state = jnp.einsum(
        "aij,ab->aibj", earlier[:, :HD, :], eye, precision=lax.Precision.HIGHEST
    ).reshape(width, width)
    earlier_sum = earlier[:, HD, :].reshape(width)

    prefix_state = earlier_state[None] + jnp.cumsum(frame_state, axis=0)
    prefix_sum = earlier_sum[None] + jnp.cumsum(frame_sum, axis=0)
    state_round = prefix_state.astype(jnp.bfloat16)
    sum_round = prefix_sum.astype(jnp.bfloat16)
    sum_matrix = jnp.where(same_head[None], sum_round[:, :, None], jnp.zeros((), jnp.bfloat16))
    numerator = jnp.einsum(
        "fti,fij->ftj", query_pos, state_round, preferred_element_type=jnp.float32
    )
    denominator = (
        jnp.einsum("fti,fij->ftj", query_pos, sum_matrix, preferred_element_type=jnp.float32)
        + EPSILON
    )
    return (numerator / denominator).astype(jnp.bfloat16).reshape(length, width)


def _project(attended, weights, shares, residual, frame_gate, nf, ng):
    rows_here = residual.shape[0]
    head_pos = lax.axis_index("heads")
    if rows_here <= FRAME_TOK and FRAME_TOK % rows_here == 0:
        gate_rows = lax.dynamic_slice_in_dim(
            frame_gate, (head_pos * rows_here) // FRAME_TOK, 1, axis=0
        )
    else:
        row_frame = (head_pos * rows_here + jnp.arange(rows_here, dtype=jnp.int32)) // FRAME_TOK
        gate_rows = jnp.take(frame_gate, row_frame, axis=0)
    token_rows = lax.all_to_all(attended, "heads", split_axis=0, concat_axis=1, tiled=True)
    nparts = 2 * ng
    depth = weights.shape[0]
    sub = depth // (nf * nparts)
    j = lax.axis_index("frames")
    block = jnp.remainder(j - jnp.arange(nf, dtype=jnp.int32), nf)
    order = (block[:, None] * nparts + shares[None, :]).reshape(-1)
    source = (order[:, None] * sub + jnp.arange(sub, dtype=jnp.int32)[None, :]).reshape(-1)
    pick = (jnp.arange(depth, dtype=jnp.int32)[:, None] == source[None, :]).astype(jnp.bfloat16)
    matched = jnp.dot(token_rows, pick, preferred_element_type=jnp.float32).astype(jnp.bfloat16)
    projected = jnp.dot(matched, weights, preferred_element_type=jnp.float32)
    return (residual.astype(jnp.float32) + gate_rows * projected).astype(jnp.bfloat16)


def solution(mesh):
    nf = mesh.shape["frames"]
    nh = mesh.shape["heads"]
    ng = mesh.shape["groups"]
    in_specs = (
        P(("groups", "frames"), "heads"),
        P(("groups", "frames"), "heads"),
        P(("groups", "frames"), "heads"),
        P(("groups", "frames", "heads"), None),
        P("frames", None),
        P(("groups", "frames"), None),
    )
    out_specs = P(("groups", "frames", "heads"), None)
    return jax.shard_map(
        make_per_device(nf, nh, ng), mesh=mesh, in_specs=in_specs, out_specs=out_specs,
        check_vma=False,
    )
```

profile of v0, /device:TPU:28, one launch (start us, length us, event | category | flops | bytes accessed | tf_op | source)
XLA Modules:
  0.0 90.1 jit_solution(18056928478249002316)
XLA Ops:
  0.0 1.8 %constant_dynamic-update-slice_fusion.3 = (bf16[896,2240]{1,0:T(8,128)(2,1)}, bf16[56,2240]{1,0:T(8,128)(2,1)}) fusion(bf16[224,2240]{1,0:T(8,128)(2,1)} %param.10, s32[]{:T(128)S(6)} %select_n.80), kind=kLoop, calls=%fused_computation.61 | loop fusion | bytes 766980
  2.0 1.8 %collective-permute-start.5 = (bf16[56,2240]{1,0:T(8,128)(2,1)}, bf16[56,2240]{1,0:T(8,128)(2,1)S(1)}, u32[]{:S(2)}, u32[]{:S(2)}) collective-permute-start(bf16[56,2240]{1,0:T(8,128)(2,1)} %get-tuple-element.6), channel_id=1, source_target_pairs={{0,12},{4,0},{8,4},{12,8},{1,13},{5,1},{9,5},{13,9},{2,14},{6,2},{... | collective-permute-start | bytes 752648 | tf_op jit(solution)/shard_map/ppermute | solution.py:38
  4.1 1.2 %broadcast_maximum_fusion = bf16[2048,224]{0,1:T(8,128)(2,1)S(1)} fusion(bf16[2048,224]{0,1:T(8,128)(2,1)} %param.7), kind=kLoop, calls=%fused_computation.25 | loop fusion | flops 458752 | bytes 1835008 | tf_op jit(solution)/shard_map/max | solution.py:66
  5.4 1.4 %convert_reduce_fusion.1 = f32[224]{0:T(256)S(1)} fusion(bf16[2048,224]{0,1:T(8,128)(2,1)} %param.7), kind=kLoop, calls=%fused_computation.7 | loop fusion | flops 1376032 | bytes 918400 | tf_op jit(solution)/shard_map/reduce_sum | solution.py:77
  7.0 2.7 %fusion.32 = (f32[224,224]{1,0:T(8,128)S(1)}, f32[4,224,224]{2,1,0:T(8,128)}) fusion(bf16[28,4,8,512]{3,2,1,0:T(8,128)(2,1)} %bitcast.88, bf16[28,4,8,512]{3,2,1,0:T(8,128)(2,1)S(1)} %bitcast.81, pred[224,224]{1,0:T(8,128)(4,1)S(1)} %broadcast_compare_fusion), kind=kOutput, calls=%fused_computation.80 | convolution fusion | flops 205872128 | bytes 2888704 | tf_op jit(solution)/shard_map/fti,ftj->fij/dot_general | solution.py:71
  9.8 1.3 %collective-permute-start.2 = (f32[2,113,112]{2,1,0:T(8,128)S(1)}, f32[2,113,112]{2,1,0:T(8,128)}, u32[]{:S(2)}, u32[]{:S(2)}) collective-permute-start(f32[2,113,112]{2,1,0:T(8,128)S(1)} %pad_maximum_fusion.2), channel_id=1, source_target_pairs={{0,12},{1,13},{2,14},{3,15},{16,28},{17,29},{18,30},{19,31}} | collective-permute-start | bytes 303752 | tf_op jit(solution)/shard_map/ppermute | solution.py:17
  11.1 1.3 %collective-permute-start = (f32[2,113,112]{2,1,0:T(8,128)S(1)}, f32[2,113,112]{2,1,0:T(8,128)}, u32[]{:S(2)}, u32[]{:S(2)}) collective-permute-start(f32[2,113,112]{2,1,0:T(8,128)S(1)} %pad_maximum_fusion.2), channel_id=1, source_target_pairs={{0,4},{4,8},{8,12},{1,5},{5,9},{9,13},{2,6},{6,10},{10,14},{3,7},{... | collective-permute-start | bytes 303752 | tf_op jit(solution)/shard_map/ppermute | solution.py:17
  13.1 1.2 %broadcast_maximum_fusion.1 = bf16[2048,224]{0,1:T(8,128)(2,1)S(1)} fusion(bf16[2048,224]{0,1:T(8,128)(2,1)} %param.6), kind=kLoop, calls=%fused_computation.26 | loop fusion | flops 458752 | bytes 1835008 | tf_op jit(solution)/shard_map/max | solution.py:65
  15.4 0.7 dynamic-slice_dynamic-update-slice_fusion.1
  16.1 0.7 dynamic-slice_dynamic-update-slice_fusion
  17.3 7.4 %collective-permute-done.2 = f32[2,113,112]{2,1,0:T(8,128)} collective-permute-done((f32[2,113,112]{2,1,0:T(8,128)S(1)}, f32[2,113,112]{2,1,0:T(8,128)}, u32[]{:S(2)}, u32[]{:S(2)}) %collective-permute-start.2) | collective-permute-done | bytes 101280 | tf_op jit(solution)/shard_map/ppermute | solution.py:17
  24.7 1.3 %collective-permute-start.1 = (f32[2,113,112]{2,1,0:T(8,128)S(1)}, f32[2,113,112]{2,1,0:T(8,128)S(1)}, u32[]{:S(2)}, u32[]{:S(2)}) collective-permute-start(f32[2,113,112]{2,1,0:T(8,128)S(1)} %pad_maximum_fusion.2), channel_id=1, source_target_pairs={{0,8},{4,12},{1,9},{5,13},{2,10},{6,14},{3,11},{7,15},{16,24},{20,... | collective-permute-start | bytes 303752 | tf_op jit(solution)/shard_map/ppermute | solution.py:17
  26.7 0.9 reduce_window_sum.23
  27.6 9.4 %collective-permute-done.1 = f32[2,113,112]{2,1,0:T(8,128)S(1)} collective-permute-done((f32[2,113,112]{2,1,0:T(8,128)S(1)}, f32[2,113,112]{2,1,0:T(8,128)S(1)}, u32[]{:S(2)}, u32[]{:S(2)}) %collective-permute-start.1) | collective-permute-done | bytes 101280 | tf_op jit(solution)/shard_map/ppermute | solution.py:17
  36.9 1.0 %add_add_fusion = f32[2,113,112]{2,1,0:T(8,128)S(1)} fusion(f32[2,113,112]{2,1,0:T(8,128)} %collective-permute-done.2, f32[2,113,112]{2,1,0:T(8,128)} %collective-permute-done, f32[2,113,112]{2,1,0:T(8,128)S(1)} %collective-permute-done.1), kind=kLoop, calls=%fused_computation.53 | loop fusion | flops 50624 | bytes 404992 | tf_op jit(solution)/shard_map/add | solution.py:17
  38.0 2.0 %fusion.31 = (bf16[3,1,56,2240]{3,2,1,0:T(8,128)(2,1)S(1)}, bf16[3,56,2240]{2,1,0:T(8,128)(2,1)}) fusion(bf16[1,56,2240]{2,1,0:T(8,128)(2,1)S(1)} %bitcast.85, bf16[1,56,2240]{2,1,0:T(8,128)(2,1)S(1)} %bitcast.86, bf16[1,56,2240]{2,1,0:T(8,128)(2,1)} %bitcast.9), kind=kLoop, calls=%fused_computation.79 | loop fusion | flops 752640 | bytes 2257920 | tf_op jit(solution)/shard_map/stack | solution.py:44
  40.5 0.8 multiply_bitcast_fusion
  41.4 1.1 %add.141 = f32[224,224]{1,0:T(8,128)S(1)} reshape(f32[2,112,2,112]{3,2,1,0:T(2,128)} %multiply_bitcast_fusion) | data formatting | bytes 401408 | tf_op jit(solution)/shard_map/add | solution.py:92
  42.6 1.3 %fusion.5 = bf16[4,224,224]{2,1,0:T(8,128)(2,1)S(1)} fusion(f32[4,224,224]{2,1,0:T(8,128)} %get-tuple-element.12, f32[224,224]{1,0:T(8,128)S(1)} %add.141), kind=kOutput, calls=%fused_computation.13 | output fusion | flops 1003520 | bytes 1404928 | tf_op jit(solution)/shard_map/jit(cumsum)/reduce_window_sum | solution.py:92
  43.8 1.7 %fusion.11 = f32[4,512,224]{1,2,0:T(8,128)} fusion(bf16[4,224,224]{2,1,0:T(8,128)(2,1)S(1)} %fusion.5, bf16[28,4,8,512]{3,2,1,0:T(8,128)(2,1)S(1)} %bitcast.82), kind=kOutput, calls=%fused_computation.19 | convolution fusion | flops 205520896 | bytes 3153920 | tf_op jit(solution)/shard_map/fti,fij->ftj/dot_general | solution.py:97
  45.6 12.8 %collective-permute-done.6 = bf16[3,56,2240]{2,1,0:T(8,128)(2,1)S(1)} collective-permute-done((bf16[3,56,2240]{2,1,0:T(8,128)(2,1)}, bf16[3,56,2240]{2,1,0:T(8,128)(2,1)S(1)}, u32[]{:S(2)}, u32[]{:S(2)}) %collective-permute-start.6) | collective-permute-done | bytes 752672 | tf_op jit(solution)/shard_map/ppermute | solution.py:41
  58.4 1.3 %pad_maximum_fusion = bf16[3,2,56,2240]{3,2,1,0:T(8,128)(2,1)} fusion(bf16[3,1,56,2240]{3,2,1,0:T(8,128)(2,1)S(1)} %bitcast.84, bf16[3,1,56,2240]{3,2,1,0:T(8,128)(2,1)S(1)} %get-tuple-element.7), kind=kLoop, calls=%fused_computation.9 | loop fusion | flops 752640 | bytes 3010560 | tf_op jit(solution)/shard_map/stack | solution.py:44
  59.7 1.6 %add_convert_fusion = bf16[4,224]{0,1:T(8,128)(2,1)} fusion(f32[4,224]{0,1:T(8,128)} %reduce_window_sum.23, f32[224]{0:T(256)S(1)} %add.144), kind=kLoop, calls=%fused_computation.54 | loop fusion | flops 1792 | bytes 6272 | tf_op jit(solution)/shard_map/convert_element_type | solution.py:95
  61.3 0.9 copy.18
  62.2 3.2 %divide_convert_fusion = bf16[4,512,224]{1,2,0:T(8,128)(2,1)} fusion(f32[4,512,224]{1,2,0:T(8,128)} %fusion.11, bf16[28,4,8,512]{3,2,1,0:T(8,128)(2,1)S(1)} %bitcast.83, pred[224,224]{1,0:T(8,128)(4,1)} %copy-done.3, bf16[4,224]{1,0:T(4,128)(2,1)S(1)} %copy.18), kind=kOutput, calls=%fused_computation.5 | convolution fusion | flops 207097856 | bytes 3721984 | tf_op jit(solution)/shard_map/fti,fij->ftj/dot_general | solution.py:101
  65.4 3.6 %all-to-all-start = ((bf16[4,512,224]{1,2,0:T(8,128)(2,1)}), bf16[4,512,224]{1,2,0:T(8,128)(2,1)S(1)}, u32[]{:S(2)}, u32[]{:S(2)}) async-start(bf16[4,512,224]{1,2,0:T(8,128)(2,1)} %divide_convert_fusion), calls=%async_computation | async-start | bytes 1835008 | tf_op jit(solution)/shard_map/all_to_all | solution.py:117
  69.0 1.7 %constant_dynamic-update-slice_fusion.2 = bf16[896,2240]{1,0:T(8,128)(2,1)} fusion(bf16[896,2240]{1,0:T(8,128)(2,1)} %dynamic-slice_dynamic-update-slice_fusion, bf16[56,2240]{1,0:T(8,128)(2,1)} %collective-permute-done.3), kind=kLoop, calls=%fused_computation.60 | loop fusion | bytes 516096
  72.9 1.7 %constant_dynamic-update-slice_fusion.1 = bf16[896,2240]{1,0:T(8,128)(2,1)} fusion(bf16[896,2240]{1,0:T(8,128)(2,1)} %fusion.23, bf16[56,2240]{1,0:T(8,128)(2,1)} %copy-done.2), kind=kLoop, calls=%fused_computation.59 | loop fusion | bytes 516096
  76.7 0.7 constant_dynamic-update-slice_fusion
  78.2 0.7 fusion.18
  79.7 2.4 %all-to-all-done = bf16[4,512,224]{1,2,0:T(8,128)(2,1)S(1)} async-done(((bf16[4,512,224]{1,2,0:T(8,128)(2,1)}), bf16[4,512,224]{1,2,0:T(8,128)(2,1)S(1)}, u32[]{:S(2)}, u32[]{:S(2)}) %all-to-all-start) | async-done | bytes 917536 | tf_op jit(solution)/shard_map/all_to_all | solution.py:117
  82.0 8.1 %fusion.1 = bf16[512,2240]{0,1:T(8,128)(2,1)} fusion(bf16[896,2240]{1,0:T(8,128)(2,1)} %fusion.17, bf16[512,2240]{0,1:T(8,128)(2,1)} %param.9, f32[2240]{0:T(1024)S(1)} %dynamic-slice_reduce_fusion, bf16[512,896]{0,1:T(8,128)(2,1)S(1)} %bitcast.87, s32[896]{0:T(1024)S(1)} %copy-done.4), kind=kOutput, calls=%fused_computation.2 | convolution fusion | flops 2883141632 | bytes 9531648 | tf_op jit(solution)/shard_map/dot_general | solution.py:127
  (45 shorter events, 10.1 us)
Async XLA Ops:
  0.0 27.5 %copy-start = (f32[4,2240]{1,0:T(4,128)S(1)}, f32[4,2240]{1,0:T(4,128)}, u32[]{:S(2)}) copy-start(f32[4,2240]{1,0:T(4,128)} %param.11) | copy-start | bytes 107524
  1.8 36.2 %collective-permute-start.3 = (bf16[56,2240]{1,0:T(8,128)(2,1)}, bf16[56,2240]{1,0:T(8,128)(2,1)}, u32[]{:S(2)}, u32[]{:S(2)}) collective-permute-start(bf16[56,2240]{1,0:T(8,128)(2,1)} %get-tuple-element.6), channel_id=1, source_target_pairs={{0,4},{4,8},{8,12},{12,0},{1,5},{5,9},{9,13},{13,1},{2,6},{6,10},{... | collective-permute-start | bytes 752648 | tf_op jit(solution)/shard_map/ppermute | solution.py:38
  2.0 36.0 %collective-permute-start.5 = (bf16[56,2240]{1,0:T(8,128)(2,1)}, bf16[56,2240]{1,0:T(8,128)(2,1)S(1)}, u32[]{:S(2)}, u32[]{:S(2)}) collective-permute-start(bf16[56,2240]{1,0:T(8,128)(2,1)} %get-tuple-element.6), channel_id=1, source_target_pairs={{0,12},{4,0},{8,4},{12,8},{1,13},{5,1},{9,5},{13,9},{2,14},{6,2},{... | collective-permute-start | bytes 752648 | tf_op jit(solution)/shard_map/ppermute | solution.py:38
  3.8 34.2 %collective-permute-start.4 = (bf16[56,2240]{1,0:T(8,128)(2,1)}, bf16[56,2240]{1,0:T(8,128)(2,1)S(1)}, u32[]{:S(2)}, u32[]{:S(2)}) collective-permute-start(bf16[56,2240]{1,0:T(8,128)(2,1)} %get-tuple-element.6), channel_id=1, source_target_pairs={{0,8},{4,12},{8,0},{12,4},{1,9},{5,13},{9,1},{13,5},{2,10},{6,14},... | collective-permute-start | bytes 752648 | tf_op jit(solution)/shard_map/ppermute | solution.py:38
  6.8 7.9 %copy-start.1 = (bf16[224,2240]{1,0:T(8,128)(2,1)S(1)}, bf16[224,2240]{1,0:T(8,128)(2,1)}, u32[]{:S(2)}) copy-start(bf16[224,2240]{1,0:T(8,128)(2,1)} %param.10) | copy-start | bytes 3010564
  6.9 2.8 %copy-start.3 = (pred[224,224]{1,0:T(8,128)(4,1)}, pred[224,224]{1,0:T(8,128)(4,1)S(1)}, u32[]{:S(2)}) copy-start(pred[224,224]{1,0:T(8,128)(4,1)S(1)} %broadcast_compare_fusion) | copy-start | bytes 150532
  9.8 14.9 %collective-permute-start.2 = (f32[2,113,112]{2,1,0:T(8,128)S(1)}, f32[2,113,112]{2,1,0:T(8,128)}, u32[]{:S(2)}, u32[]{:S(2)}) collective-permute-start(f32[2,113,112]{2,1,0:T(8,128)S(1)} %pad_maximum_fusion.2), channel_id=1, source_target_pairs={{0,12},{1,13},{2,14},{3,15},{16,28},{17,29},{18,30},{19,31}} | collective-permute-start | bytes 303752 | tf_op jit(solution)/shard_map/ppermute | solution.py:17
  11.1 16.5 %collective-permute-start = (f32[2,113,112]{2,1,0:T(8,128)S(1)}, f32[2,113,112]{2,1,0:T(8,128)}, u32[]{:S(2)}, u32[]{:S(2)}) collective-permute-start(f32[2,113,112]{2,1,0:T(8,128)S(1)} %pad_maximum_fusion.2), channel_id=1, source_target_pairs={{0,4},{4,8},{8,12},{1,5},{5,9},{9,13},{2,6},{6,10},{10,14},{3,7},{... | collective-permute-start | bytes 303752 | tf_op jit(solution)/shard_map/ppermute | solution.py:17
  24.7 12.3 %collective-permute-start.1 = (f32[2,113,112]{2,1,0:T(8,128)S(1)}, f32[2,113,112]{2,1,0:T(8,128)S(1)}, u32[]{:S(2)}, u32[]{:S(2)}) collective-permute-start(f32[2,113,112]{2,1,0:T(8,128)S(1)} %pad_maximum_fusion.2), channel_id=1, source_target_pairs={{0,8},{4,12},{1,9},{5,13},{2,10},{6,14},{3,11},{7,15},{16,24},{20,... | collective-permute-start | bytes 303752 | tf_op jit(solution)/shard_map/ppermute | solution.py:17
  38.0 20.4 %copy-start.2 = (bf16[56,2240]{1,0:T(8,128)(2,1)}, bf16[56,2240]{1,0:T(8,128)(2,1)S(1)}, u32[]{:S(2)}) copy-start(bf16[56,2240]{1,0:T(8,128)(2,1)S(1)} %collective-permute-done.4) | copy-start | bytes 752644
  40.0 18.4 %collective-permute-start.6 = (bf16[3,56,2240]{2,1,0:T(8,128)(2,1)}, bf16[3,56,2240]{2,1,0:T(8,128)(2,1)S(1)}, u32[]{:S(2)}, u32[]{:S(2)}) collective-permute-start(bf16[3,56,2240]{2,1,0:T(8,128)(2,1)} %get-tuple-element.8), channel_id=1, source_target_pairs={{0,16},{16,0},{1,17},{17,1},{2,18},{18,2},{3,19},{19,3},{4,20},{20... | collective-permute-start | bytes 2257928 | tf_op jit(solution)/shard_map/ppermute | solution.py:41
  59.7 11.7 %collective-permute-start.7 = (bf16[3,2,56,2240]{3,2,1,0:T(8,128)(2,1)}, bf16[3,2,56,2240]{3,2,1,0:T(8,128)(2,1)S(1)}, u32[]{:S(2)}, u32[]{:S(2)}) collective-permute-start(bf16[3,2,56,2240]{3,2,1,0:T(8,128)(2,1)} %pad_maximum_fusion), channel_id=1, source_target_pairs={{0,1},{1,0},{2,3},{3,2},{4,5},{5,4},{6,7},{7,6},{8,9},{9,8},{10,11... | collective-permute-start | bytes 4515848 | tf_op jit(solution)/shard_map/ppermute | solution.py:45
  65.4 16.6 %copy-start.4 = (s32[896]{0:T(1024)S(1)}, s32[896]{0:T(1024)}, u32[]{:S(2)}) copy-start(s32[896]{0:T(1024)} %add.163) | copy-start | bytes 10756
  65.4 16.6 %all-to-all-start = ((bf16[4,512,224]{1,2,0:T(8,128)(2,1)}), bf16[4,512,224]{1,2,0:T(8,128)(2,1)S(1)}, u32[]{:S(2)}, u32[]{:S(2)}) async-start(bf16[4,512,224]{1,2,0:T(8,128)(2,1)} %divide_convert_fusion), calls=%async_computation | async-start | bytes 1835008 | tf_op jit(solution)/shard_map/all_to_all | solution.py:117
where the time goes:
time: 90.8 us; the launch traced here: 90.1 us
  waiting for transfers between devices  31.9 us (35%)
  local copies, waits for them, and re-layouts  18.3 us (20%)
  matrix products  15.7 us (17%)
  other arithmetic  13.6 us (15%)
  starting transfers between devices  10.4 us (11%)
    ppermute x3, waiting for transfers between devices, _exclusive_prefix(): lax.ppermute(x, 'frames', [(i, i + d) for i in range(nf - d)])  16.7 us
    unnamed x25, local copies, waits for them, and re-layouts  13.9 us
    ppermute x1, waiting for transfers between devices, _ring_out_proj(): lax.ppermute(fetched, 'groups', [(a, (a + s) % ng) for a in range(ng)])  12.8 us
    dot_general x1, matrix products, _project(): projected = jnp.dot(matched, weights, preferred_element_type=jnp.float32)  8.06 us
    ppermute x3, starting transfers between devices, _exclusive_prefix(): lax.ppermute(x, 'frames', [(i, i + d) for i in range(nf - d)])  3.86 us
    all_to_all x1, starting transfers between devices, _project(): lax.all_to_all(attended, 'heads', split_axis=0, concat_axis=1, tiled=True)  3.64 us
    another operation x2, other arithmetic, _ring_out_proj(): mine = jnp.stack(from_groups, axis=1)  3.35 us
    dot_general x1, matrix products, _attend(): jnp.einsum('fti,fij->ftj', query_pos, sum_matrix, preferred_element_type=...  3.17 us
  transfers between devices with their start and end apart: 9, of which 4 were waited for; matrix products, arithmetic and copies ran while one was open for 38% of the time, Pallas kernels for 0%

commit v1 on v0

--- a/solution.py
+++ b/solution.py
@@ -24,35 +24,26 @@
     return y
 
 
-def _ring_out_proj(out_proj, nf, nh, ng):
-    rows, _ = out_proj.shape
+def _gather_out_proj(out_proj, nf, nh, ng):
+    rows, cols = out_proj.shape
     sub = rows // (2 * ng)
     g = lax.axis_index("groups")
     core = lax.axis_index("heads") % 2
-    shares = [jnp.remainder(g - s, ng) * 2 + core for s in range(ng)]
-    shares += [jnp.remainder(g - s, ng) * 2 + 1 - core for s in range(ng)]
-    pieces = [lax.dynamic_slice_in_dim(out_proj, share * sub, sub, axis=0) for share in shares]
-    swap = [(a, a ^ 1) for a in range(nh)]
-    fetched = []
-    for t in range(1, nf):
-        fetched.append(lax.ppermute(pieces[0], "frames", [(i, (i + t) % nf) for i in range(nf)]))
-    fetched = jnp.stack(fetched)
-    from_groups = [fetched] + [
-        lax.ppermute(fetched, "groups", [(a, (a + s) % ng) for a in range(ng)])
-        for s in range(1, ng)
-    ]
-    mine = jnp.stack(from_groups, axis=1)
-    theirs = lax.ppermute(mine, "heads", swap)
-    for t in range(nf - 1):
-        pieces += [mine[t, s] for s in range(ng)] + [theirs[t, s] for s in range(ng)]
-    return jnp.concatenate(pieces, axis=0), jnp.stack(shares)
+    mine = lax.dynamic_slice_in_dim(out_proj, (2 * g + core) * sub, sub, axis=0)
+    gathered = lax.all_gather(mine, ("groups", "frames"), axis=0)
+    theirs = lax.ppermute(gathered, "heads", [(a, a ^ 1) for a in range(nh)])
+    weights = jnp.concatenate([gathered, theirs], axis=0).reshape(2 * ng * nf * sub, cols)
+    group_of = jnp.repeat(jnp.arange(ng, dtype=jnp.int32), nf)
+    block = jnp.tile(jnp.arange(nf, dtype=jnp.int32), 2 * ng)
+    share = jnp.concatenate([2 * group_of + core, 2 * group_of + 1 - core])
+    return weights, block, share
 
 
 def make_per_device(nf, nh, ng):
     def per_device(query_heads, key_heads, value_heads, residual, out_proj, frame_gate):
-        weights, shares = _ring_out_proj(out_proj, nf, nh, ng)
+        weights, block, share = _gather_out_proj(out_proj, nf, nh, ng)
         attended = _attend(query_heads, key_heads, value_heads, nf)
-        return _project(attended, weights, shares, residual, frame_gate, nf, ng)
+        return _project(attended, weights, block, share, residual, frame_gate, nf, ng)
 
     return per_device
 
@@ -104,7 +95,7 @@
     return (numerator / denominator).astype(jnp.bfloat16).reshape(length, width)
 
 
-def _project(attended, weights, shares, residual, frame_gate, nf, ng):
+def _project(attended, weights, block, share, residual, frame_gate, nf, ng):
     rows_here = residual.shape[0]
     head_pos = lax.axis_index("heads")
     if rows_here <= FRAME_TOK and FRAME_TOK % rows_here == 0:
@@ -115,13 +106,10 @@
         row_frame = (head_pos * rows_here + jnp.arange(rows_here, dtype=jnp.int32)) // FRAME_TOK
         gate_rows = jnp.take(frame_gate, row_frame, axis=0)
     token_rows = lax.all_to_all(attended, "heads", split_axis=0, concat_axis=1, tiled=True)
-    nparts = 2 * ng
     depth = weights.shape[0]
-    sub = depth // (nf * nparts)
-    j = lax.axis_index("frames")
-    block = jnp.remainder(j - jnp.arange(nf, dtype=jnp.int32), nf)
-    order = (block[:, None] * nparts + shares[None, :]).reshape(-1)
-    source = (order[:, None] * sub + jnp.arange(sub, dtype=jnp.int32)[None, :]).reshape(-1)
+    sub = depth // (nf * 2 * ng)
+    row_of = (block * (2 * ng) + share) * sub
+    source = (row_of[:, None] + jnp.arange(sub, dtype=jnp.int32)[None, :]).reshape(-1)
     pick = (jnp.arange(depth, dtype=jnp.int32)[:, None] == source[None, :]).astype(jnp.bfloat16)
     matched = jnp.dot(token_rows, pick, preferred_element_type=jnp.float32).astype(jnp.bfloat16)
     projected = jnp.dot(matched, weights, preferred_element_type=jnp.float32)

time: 90.8 us -> 104 us (1.15)
  the two profiles are of different devices: /device:TPU:28 before, /device:TPU:0 now
where the time goes in v1:
time: 104 us
  waiting for transfers between devices  47.3 us (45%)
  starting transfers between devices  14.9 us (14%)
  between operations  13.6 us (13%)
  matrix products  12.8 us (12%)
  other arithmetic  11 us (11%)
  local copies, waits for them, and re-layouts  4.27 us (4%)
    all_gather x1, waiting for transfers between devices, _gather_out_proj(): gathered = lax.all_gather(mine, ('groups', 'frames'), axis=0)  39.7 us
    ppermute x3, starting transfers between devices, _exclusive_prefix(): lax.ppermute(x, 'frames', [(i, i + d) for i in range(nf - d)])  11.4 us
    dot_general x1, matrix products, _project(): projected = jnp.dot(matched, weights, preferred_element_type=jnp.float32)  8.06 us
    all_to_all x1, waiting for transfers between devices, _project(): lax.all_to_all(attended, 'heads', split_axis=0, concat_axis=1, tiled=True)  7.49 us
    concatenate x1, other arithmetic, _gather_out_proj(): jnp.concatenate([gathered, theirs], axis=0).reshape(2 * ng * nf * sub, cols)  4.51 us
    all_to_all x1, starting transfers between devices, _project(): lax.all_to_all(attended, 'heads', split_axis=0, concat_axis=1, tiled=True)  3.51 us
    dot_general x1, matrix products, _attend(): jnp.einsum('fti,ftj->fij', key_pos, value_frames, preferred_element_type=...  2.57 us
  transfers between devices with their start and end apart: 6, of which 2 were waited for; matrix products, arithmetic and copies ran while one was open for 17% of the time, Pallas kernels for 0%

profile of v1, /device:TPU:0, one launch (start us, length us, event | category | flops | bytes accessed | tf_op | source)
XLA Modules:
  0.0 103.8 jit_solution(5973021331225690483)
XLA Ops:
  6.5 1.2 %copy-done = bf16[224,2240]{1,0:T(8,128)(2,1)S(1)} copy-done((bf16[224,2240]{1,0:T(8,128)(2,1)S(1)}, bf16[224,2240]{1,0:T(8,128)(2,1)}, u32[]{:S(2)}) %copy-start) | copy-done | bytes 1003544
  7.8 0.7 constant_dynamic-slice_fusion
  8.5 1.4 %convert_reduce_fusion.1 = f32[224]{0:T(256)S(1)} fusion(bf16[2048,224]{0,1:T(8,128)(2,1)} %param.7), kind=kLoop, calls=%fused_computation.8 | loop fusion | flops 1376032 | bytes 918400 | tf_op jit(solution)/shard_map/reduce_sum | solution.py:68
  9.9 0.1 reshape.145
  10.0 0.1 broadcast_compare_fusion
  10.2 2.6 %fusion.22 = (f32[224,224]{1,0:T(8,128)S(1)}, f32[4,224,224]{2,1,0:T(8,128)}) fusion(bf16[28,4,8,512]{3,2,1,0:T(8,128)(2,1)} %bitcast.42, bf16[28,4,8,512]{3,2,1,0:T(8,128)(2,1)S(1)} %bitcast.36, pred[224,224]{1,0:T(8,128)(4,1)S(1)} %broadcast_compare_fusion), kind=kOutput, calls=%fused_computation.52 | convolution fusion | flops 205872128 | bytes 2888704 | tf_op jit(solution)/shard_map/fti,ftj->fij/dot_general | solution.py:62
  12.9 5.0 %collective-permute-start = (f32[2,113,112]{2,1,0:T(8,128)S(1)}, f32[2,113,112]{2,1,0:T(8,128)S(1)}, u32[]{:S(2)}, u32[]{:S(2)}) collective-permute-start(f32[2,113,112]{2,1,0:T(8,128)S(1)} %pad_maximum_fusion.1), channel_id=1, source_target_pairs={{0,4},{4,8},{8,12},{1,5},{5,9},{9,13},{2,6},{6,10},{10,14},{3,7},{... | collective-permute-start | bytes 303752 | tf_op jit(solution)/shard_map/ppermute | solution.py:17
  17.9 4.5 %collective-permute-start.1 = (f32[2,113,112]{2,1,0:T(8,128)S(1)}, f32[2,113,112]{2,1,0:T(8,128)S(1)}, u32[]{:S(2)}, u32[]{:S(2)}) collective-permute-start(f32[2,113,112]{2,1,0:T(8,128)S(1)} %pad_maximum_fusion.1), channel_id=1, source_target_pairs={{0,8},{4,12},{1,9},{5,13},{2,10},{6,14},{3,11},{7,15},{16,24},{20,... | collective-permute-start | bytes 303752 | tf_op jit(solution)/shard_map/ppermute | solution.py:17
  22.4 2.0 %collective-permute-start.2 = (f32[2,113,112]{2,1,0:T(8,128)S(1)}, f32[2,113,112]{2,1,0:T(8,128)}, u32[]{:S(2)}, u32[]{:S(2)}) collective-permute-start(f32[2,113,112]{2,1,0:T(8,128)S(1)} %pad_maximum_fusion.1), channel_id=1, source_target_pairs={{0,12},{1,13},{2,14},{3,15},{16,28},{17,29},{18,30},{19,31}} | collective-permute-start | bytes 303752 | tf_op jit(solution)/shard_map/ppermute | solution.py:17
  24.3 0.7 reshape.143
  25.0 0.1 add.120
  25.1 0.1 sub.24
  25.2 0.1 mul.51
  25.3 0.4 convert_reduce_fusion
  25.7 0.9 reduce_window_sum.23
  26.6 1.2 %broadcast_maximum_fusion.1 = bf16[2048,224]{0,1:T(8,128)(2,1)S(1)} fusion(bf16[2048,224]{0,1:T(8,128)(2,1)} %param.6), kind=kLoop, calls=%fused_computation.25 | loop fusion | flops 458752 | bytes 1835008 | tf_op jit(solution)/shard_map/max | solution.py:56
  27.9 39.7 %all-gather.3.cloned.1.call-done = bf16[448,2240]{1,0:T(8,128)(2,1)} async-done(((bf16[56,2240]{1,0:T(8,128)(2,1)}), bf16[448,2240]{1,0:T(8,128)(2,1)}) %all-gather.3.cloned.1.call-update) | async-done | bytes 2007056 | tf_op jit(solution)/shard_map/all_gather | solution.py:33
  67.7 0.9 add_add_fusion
  68.6 0.1 multiply_bitcast_fusion
  68.8 0.2 add.109
  69.0 0.1 add.112
  69.0 1.0 add_convert_fusion
  70.0 0.1 copy.17
  70.1 0.1 fusion.5
  70.2 0.5 fusion.11
  70.7 1.6 %divide_convert_fusion = bf16[4,512,224]{1,2,0:T(8,128)(2,1)} fusion(f32[4,512,224]{1,2,0:T(8,128)S(1)} %fusion.11, bf16[28,4,8,512]{3,2,1,0:T(8,128)(2,1)S(1)} %bitcast.38, pred[224,224]{1,0:T(8,128)(4,1)S(1)} %broadcast_compare_fusion, bf16[4,224]{1,0:T(4,128)(2,1)S(1)} %copy.17), kind=kOutput, calls=%fused_computation.6 | convolution fusion | flops 207097856 | bytes 3721984 | tf_op jit(solution)/shard_map/fti,fij->ftj/dot_general | solution.py:92
  72.4 3.5 %all-to-all-start = ((bf16[4,512,224]{1,2,0:T(8,128)(2,1)}), bf16[4,512,224]{1,2,0:T(8,128)(2,1)S(1)}, u32[]{:S(2)}, u32[]{:S(2)}) async-start(bf16[4,512,224]{1,2,0:T(8,128)(2,1)} %divide_convert_fusion), calls=%async_computation | async-start | bytes 1835008 | tf_op jit(solution)/shard_map/all_to_all | solution.py:108
  76.0 0.1 add.126
  76.1 0.8 dynamic-slice_reduce_fusion
  76.9 4.5 %pad_maximum_fusion = bf16[16,56,2240]{2,1,0:T(8,128)(2,1)} fusion(bf16[8,56,2240]{2,1,0:T(8,128)(2,1)} %collective-permute-done.3, bf16[8,56,2240]{2,1,0:T(8,128)(2,1)} %bitcast.40), kind=kLoop, calls=%fused_computation.3 | loop fusion | flops 2007040 | bytes 8028160 | tf_op jit(solution)/shard_map/concatenate | solution.py:35
  81.4 7.5 %all-to-all-done = bf16[4,512,224]{1,2,0:T(8,128)(2,1)S(1)} async-done(((bf16[4,512,224]{1,2,0:T(8,128)(2,1)}), bf16[4,512,224]{1,2,0:T(8,128)(2,1)S(1)}, u32[]{:S(2)}, u32[]{:S(2)}) %all-to-all-start) | async-done | bytes 917536 | tf_op jit(solution)/shard_map/all_to_all | solution.py:108
  88.9 8.1 %fusion.1 = bf16[512,2240]{0,1:T(8,128)(2,1)} fusion(bf16[896,2240]{1,0:T(8,128)(2,1)} %bitcast.35, bf16[512,2240]{0,1:T(8,128)(2,1)} %param.9, f32[2240]{0:T(1024)S(1)} %dynamic-slice_reduce_fusion, bf16[512,896]{0,1:T(8,128)(2,1)S(1)} %bitcast.41, s32[896]{0:T(1024)S(1)} %add.126), kind=kOutput, calls=%fused_computation.2 | convolution fusion | flops 2883141632 | bytes 9531648 | tf_op jit(solution)/shard_map/dot_general | solution.py:115
  (23 shorter events, 0.4 us)
Async XLA Ops:
  6.5 1.2 %copy-start = (bf16[224,2240]{1,0:T(8,128)(2,1)S(1)}, bf16[224,2240]{1,0:T(8,128)(2,1)}, u32[]{:S(2)}) copy-start(bf16[224,2240]{1,0:T(8,128)(2,1)} %param.10) | copy-start | bytes 3010564
  6.5 3.6 %copy-start.1 = (bf16[2048,224]{0,1:T(8,128)(2,1)S(1)}, bf16[2048,224]{0,1:T(8,128)(2,1)}, u32[]{:S(2)}) copy-start(bf16[2048,224]{0,1:T(8,128)(2,1)} %param.7) | copy-start | bytes 2752516
  6.5 61.1 %all-gather.3.cloned.1.call-start = ((), (), s32[]{:S(2)}) async-start(), calls=%async_computation.1 | async-start | bytes 2322432 | tf_op jit(solution)/shard_map/all_gather | solution.py:33
  12.9 54.8 %collective-permute-start = (f32[2,113,112]{2,1,0:T(8,128)S(1)}, f32[2,113,112]{2,1,0:T(8,128)S(1)}, u32[]{:S(2)}, u32[]{:S(2)}) collective-permute-start(f32[2,113,112]{2,1,0:T(8,128)S(1)} %pad_maximum_fusion.1), channel_id=1, source_target_pairs={{0,4},{4,8},{8,12},{1,5},{5,9},{9,13},{2,6},{6,10},{10,14},{3,7},{... | collective-permute-start | bytes 303752 | tf_op jit(solution)/shard_map/ppermute | solution.py:17
  17.9 49.8 %collective-permute-start.1 = (f32[2,113,112]{2,1,0:T(8,128)S(1)}, f32[2,113,112]{2,1,0:T(8,128)S(1)}, u32[]{:S(2)}, u32[]{:S(2)}) collective-permute-start(f32[2,113,112]{2,1,0:T(8,128)S(1)} %pad_maximum_fusion.1), channel_id=1, source_target_pairs={{0,8},{4,12},{1,9},{5,13},{2,10},{6,14},{3,11},{7,15},{16,24},{20,... | collective-permute-start | bytes 303752 | tf_op jit(solution)/shard_map/ppermute | solution.py:17
  22.4 45.3 %collective-permute-start.2 = (f32[2,113,112]{2,1,0:T(8,128)S(1)}, f32[2,113,112]{2,1,0:T(8,128)}, u32[]{:S(2)}, u32[]{:S(2)}) collective-permute-start(f32[2,113,112]{2,1,0:T(8,128)S(1)} %pad_maximum_fusion.1), channel_id=1, source_target_pairs={{0,12},{1,13},{2,14},{3,15},{16,28},{17,29},{18,30},{19,31}} | collective-permute-start | bytes 303752 | tf_op jit(solution)/shard_map/ppermute | solution.py:17
  25.3 44.8 %copy-start.2 = (f32[4,224,224]{2,1,0:T(8,128)S(1)}, f32[4,224,224]{2,1,0:T(8,128)}, u32[]{:S(2)}) copy-start(f32[4,224,224]{2,1,0:T(8,128)} %get-tuple-element.8) | copy-start | bytes 2408452
  67.6 9.2 %collective-permute-start.3 = (bf16[8,56,2240]{2,1,0:T(8,128)(2,1)}, bf16[8,56,2240]{2,1,0:T(8,128)(2,1)}, u32[]{:S(2)}, u32[]{:S(2)}) collective-permute-start(bf16[8,56,2240]{2,1,0:T(8,128)(2,1)} %bitcast.39), channel_id=1, source_target_pairs={{0,1},{1,0},{2,3},{3,2},{4,5},{5,4},{6,7},{7,6},{8,9},{9,8},{10,11... | collective-permute-start | bytes 6021128 | tf_op jit(solution)/shard_map/ppermute | solution.py:34
  72.4 16.5 %all-to-all-start = ((bf16[4,512,224]{1,2,0:T(8,128)(2,1)}), bf16[4,512,224]{1,2,0:T(8,128)(2,1)S(1)}, u32[]{:S(2)}, u32[]{:S(2)}) async-start(bf16[4,512,224]{1,2,0:T(8,128)(2,1)} %divide_convert_fusion), calls=%async_computation | async-start | bytes 1835008 | tf_op jit(solution)/shard_map/all_to_all | solution.py:108
Sparse Core Ops, SparseCore 0:
  9.4 58.1 all-gather.2
